TPU v7x, 512 devices: a whole 4x8x8 slice. The times are simulated.
512 devices in a mesh: segment: 16 (over y, z_lo), ctx: 32 (over x, z_hi, core).
Axes of the slice: x: 4, y: 8, z: 8 (z_hi: 4, z_lo: 2; z = z_hi * 2 + z_lo), core: 2. Of those that a mesh axis runs over, the one named last changes fastest.
Arguments:
- perturbed_frame_activation: bfloat16 [2, 256, 1536], P(None, 'ctx'), may hold values from -8 to 8
- inbound_activation: bfloat16 [16, 256, 1536], P('segment', 'ctx'), may hold values from -6 to 6
- section_block_indices: int32 [16], P('segment'), may hold values from 1 to 2, as said below
- tile_arrival_permutation: int32 [2], replicated, may hold values from 0 to 1, each once
- adaptive_shifting: float32 [16, 2, 1536], P('segment'), may hold values from -6 to 6
- adaptive_scaling: float32 [16, 2, 1536], P('segment'), may hold values from -4 to 4
- tier_query_factor: float32 [16, 2, 1536], P('segment'), may hold values from 0.3 to 3
- tier_skip_coefficient: float32 [16, 2, 1536], P('segment'), may hold values from -12 to 12
- earlier_step_lookup_matrix: bfloat16 [16, 2, 2, 256, 1536], P('segment', None, None, 'ctx'), may hold values from -10.5 to 10.5
- earlier_step_content_matrix: bfloat16 [16, 2, 2, 256, 1536], P('segment', None, None, 'ctx'), may hold values from -3 to 3
Outputs:
- section_out: bfloat16 [16, 2, 256, 1536], P('segment', None, 'ctx')
Inputs may be any that keep to these rules, and one draw needn't show every extreme that they name: `section_block_indices`: some segment uses exactly 2 slots and some exactly 1. `tile_arrival_permutation`: each patch once.
All inputs are finite; a program needn't handle non-finite values.
Results may differ from a plain program's by a relative error of at most 0.013.
Values may be sent and summed in bfloat16 or wider, within the bound.
No kernel may reach another device: no remote copies, remote signals or barrier semaphores. Data moves between devices by JAX's collectives and lax.ppermute only.
A program may use at most 64 MiB of HBM per device.

v0:
```python
import math
import jax
import jax.numpy as jnp
from jax import lax
from jax.sharding import Mesh
from jax.sharding import PartitionSpec as P

HD = 128
EPSILON = 1e-06
HEAD_AXIS = "cx"
TOKEN_AXES = ("cz", "cc")
CTX_AXES = ("cx", "cz", "cc")


def head_norm(values):
    return values * lax.rsqrt(jnp.mean(values * values, axis=-1, keepdims=True) + EPSILON)


def to_head_groups(rows, groups):
    *lead, n, width = rows.shape
    split = rows.reshape(*lead, n, groups, width // groups)
    return jnp.moveaxis(split, -2, 0)


def per_device(
    perturbed_frame_activation,
    inbound_activation,
    section_block_indices,
    tile_arrival_permutation,
    adaptive_shifting,
    adaptive_scaling,
    tier_query_factor,
    tier_skip_coefficient,
    earlier_step_lookup_matrix,
    earlier_step_content_matrix,
):
    segment = lax.axis_index("segment")
    patch_count = tile_arrival_permutation.shape[0]
    rows = inbound_activation.shape[1]
    width = inbound_activation.shape[2]
    heads = width // HD
    groups = lax.axis_size(HEAD_AXIS)
    group_width = width // groups
    group_heads = heads // groups
    slot_count = earlier_step_lookup_matrix.shape[1]
    layers_here = section_block_indices[0]
    scale = 1.0 / math.sqrt(HD)

    def gather_head_group(kv_rows):
        parts = to_head_groups(kv_rows, groups)
        mine = lax.all_to_all(parts, HEAD_AXIS, 0, 0)
        mine = jnp.moveaxis(mine, 0, -3)
        mine = mine.reshape(*mine.shape[:-3], groups * rows, group_width)
        return lax.all_gather(mine, TOKEN_AXES, axis=mine.ndim - 2, tiled=True)

    other_patch = tile_arrival_permutation[jnp.mod(1 - segment, patch_count)]
    other_k = lax.dynamic_index_in_dim(
        earlier_step_lookup_matrix[0], other_patch, 1, keepdims=False
    )
    other_v = lax.dynamic_index_in_dim(
        earlier_step_content_matrix[0], other_patch, 1, keepdims=False
    )
    other_kv = gather_head_group(jnp.stack([other_k, other_v], axis=1))

    def layer(state, tier, far_kv):
        live = layers_here > tier
        x = state.astype(jnp.float32)
        hidden = (
            x
            * lax.rsqrt(jnp.mean(x * x, axis=-1, keepdims=True) + EPSILON)
            * (1.0 + adaptive_scaling[0, tier])
            + adaptive_shifting[0, tier]
        )
        query = head_norm(hidden.reshape(rows, heads, HD)).reshape(rows, width).astype(jnp.bfloat16)
        fresh_key = (
            head_norm((hidden * tier_query_factor[0, tier]).reshape(rows, heads, HD))
            .reshape(rows, width)
            .astype(jnp.bfloat16)
        )
        fresh_value = hidden.astype(jnp.bfloat16)
        packed = to_head_groups(jnp.stack([query, fresh_key, fresh_value]), groups)
        mine = lax.all_to_all(packed, HEAD_AXIS, 0, 0)
        local_q = mine[:, 0].reshape(groups * rows, group_heads, HD)
        near_kv = jnp.moveaxis(mine[:, 1:], 0, 1).reshape(2, groups * rows, group_width)
        near_kv = lax.all_gather(near_kv, TOKEN_AXES, axis=1, tiled=True)
        keys = jnp.concatenate([near_kv[0], far_kv[0]], axis=0)
        values = jnp.concatenate([near_kv[1], far_kv[1]], axis=0)
        key_count = keys.shape[0]
        scores = (
            jnp.einsum(
                "phd,nhd->phn",
                local_q,
                keys.reshape(key_count, group_heads, HD),
                preferred_element_type=jnp.float32,
            )
            * scale
        )
        weights = jnp.exp(scores)
        total = jnp.sum(weights, axis=-1)
        numerator = jnp.einsum(
            "phn,nhd->phd",
            weights.astype(jnp.bfloat16),
            values.reshape(key_count, group_heads, HD),
            preferred_element_type=jnp.float32,
        )
        attended = (numerator / total[..., None]).reshape(groups, rows, group_width)
        back = lax.all_to_all(attended, HEAD_AXIS, 0, 0)
        back = jnp.moveaxis(back, 0, 1).reshape(rows, width)
        new_state = (x + tier_skip_coefficient[0, tier] * back).astype(jnp.bfloat16)
        return (jnp.where(live, new_state, state), near_kv)

    outcomes = []
    state = jnp.where(
        segment == 0,
        lax.dynamic_index_in_dim(
            perturbed_frame_activation, tile_arrival_permutation[0], 0, keepdims=False
        ),
        inbound_activation[0],
    )
    first_turn_kv = []
    for tier in range(slot_count):
        state, near_kv = layer(state, tier, other_kv[tier])
        first_turn_kv.append(near_kv)
    outcomes.append(state)
    for turn in range(1, patch_count):
        count = lax.axis_size("segment")
        arrived = lax.ppermute(state, "segment", [(i, i + 1) for i in range(count - 1)])
        state = jnp.where(
            segment == 0,
            lax.dynamic_index_in_dim(
                perturbed_frame_activation, tile_arrival_permutation[turn], 0, keepdims=False
            ),
            arrived,
        )
        for tier in range(slot_count):
            state, _ = layer(state, tier, first_turn_kv[tier])
        outcomes.append(state)
    return jnp.stack(outcomes)[None]


def solution(mesh):
    segments, ctx = mesh.devices.shape
    heads_mesh = Mesh(mesh.devices.reshape(segments, 4, ctx // 8, 2), ("segment",) + CTX_AXES)
    return jax.shard_map(
        per_device,
        mesh=heads_mesh,
        in_specs=(
            P(None, CTX_AXES, None),
            P("segment", CTX_AXES, None),
            P("segment"),
            P(),
            P("segment", None, None),
            P("segment", None, None),
            P("segment", None, None),
            P("segment", None, None),
            P("segment", None, None, CTX_AXES, None),
            P("segment", None, None, CTX_AXES, None),
        ),
        out_specs=P("segment", None, CTX_AXES, None),
        check_vma=False,
    )
```

profile of v0, /device:TPU:32, one launch (start us, length us, event | category | flops | bytes accessed | tf_op | source)
XLA Modules:
  0.0 178.7 jit_solution(13781949084585847155)
XLA Ops:
  0.7 0.7 fusion.130
  5.1 4.4 %all-to-all-start = ((bf16[4,3,8,384]{3,2,1,0:T(8,128)(2,1)}), bf16[4,3,8,384]{3,2,1,0:T(8,128)(2,1)S(1)}, u32[]{:S(2)}, u32[]{:S(2)}) async-start(bf16[4,3,8,384]{3,2,1,0:T(8,128)(2,1)} %maximum_bitcast_fusion.1), calls=%async_computation | async-start | bytes 147456 | tf_op jit(solution)/shard_map/all_to_all | solution.py:82
  12.4 2.8 %all-to-all-done = bf16[4,3,8,384]{3,2,1,0:T(8,128)(2,1)S(1)} async-done(((bf16[4,3,8,384]{3,2,1,0:T(8,128)(2,1)}), bf16[4,3,8,384]{3,2,1,0:T(8,128)(2,1)S(1)}, u32[]{:S(2)}, u32[]{:S(2)}) %all-to-all-start) | async-done | bytes 73760 | tf_op jit(solution)/shard_map/all_to_all | solution.py:82
  15.2 3.3 %all-to-all-start.1 = ((bf16[4,2,2,8,384]{4,3,1,2,0:T(8,128)(2,1)}), bf16[4,2,2,8,384]{4,3,1,2,0:T(8,128)(2,1)S(1)}, u32[]{:S(2)}, u32[]{:S(2)}) async-start(bf16[4,2,2,8,384]{4,3,1,2,0:T(8,128)(2,1)} %copy.78), calls=%async_computation.1 | async-start | bytes 196608 | tf_op jit(solution)/shard_map/all_to_all | solution.py:51
  18.5 20.3 %all_gather.15 = bf16[2,256,384]{2,1,0:T(8,128)(2,1)S(1)} all-gather(bf16[2,32,384]{2,1,0:T(8,128)(2,1)S(1)} %copy_bitcast_fusion.4), channel_id=1, replica_groups=mesh['segment'=16,'cx'=4,'cz'=4,'cc'=2] {'cz','cc'}, dimensions={1}, use_global_device_ids=true | all-gather | bytes 442368 | tf_op jit(solution)/shard_map/all_gather | solution.py:85
  39.6 15.5 %all_gather.16 = bf16[2,2,256,384]{3,2,1,0:T(8,128)(2,1)S(1)} all-gather(bf16[2,2,32,384]{3,2,1,0:T(8,128)(2,1)S(1)} %bitcast.189), channel_id=1, replica_groups=mesh['segment'=16,'cx'=4,'cz'=4,'cc'=2] {'cz','cc'}, dimensions={2}, use_global_device_ids=true | all-gather | bytes 884736 | tf_op jit(solution)/shard_map/all_gather | solution.py:54
  56.4 0.6 reshape.603
  57.0 4.9 %all-to-all-start.2 = ((f32[4,8,384]{2,1,0:T(8,128)}), f32[4,8,384]{2,1,0:T(8,128)S(1)}, u32[]{:S(2)}, u32[]{:S(2)}) async-start(f32[4,8,384]{2,1,0:T(8,128)} %reshape.603), calls=%async_computation.2 | async-start | bytes 98304 | tf_op jit(solution)/shard_map/all_to_all | solution.py:107
  62.6 4.8 %all-to-all-done.2 = f32[4,8,384]{2,1,0:T(8,128)S(1)} async-done(((f32[4,8,384]{2,1,0:T(8,128)}), f32[4,8,384]{2,1,0:T(8,128)S(1)}, u32[]{:S(2)}, u32[]{:S(2)}) %all-to-all-start.2) | async-done | bytes 49184 | tf_op jit(solution)/shard_map/all_to_all | solution.py:107
  68.6 3.3 %all-to-all-start.3 = ((bf16[4,3,8,384]{3,2,1,0:T(8,128)(2,1)}), bf16[4,3,8,384]{3,2,1,0:T(8,128)(2,1)S(1)}, u32[]{:S(2)}, u32[]{:S(2)}) async-start(bf16[4,3,8,384]{3,2,1,0:T(8,128)(2,1)} %maximum_bitcast_fusion.2), calls=%async_computation.3 | async-start | bytes 147456 | tf_op jit(solution)/shard_map/all_to_all | solution.py:82
  72.5 5.0 %all-to-all-done.3 = bf16[4,3,8,384]{3,2,1,0:T(8,128)(2,1)S(1)} async-done(((bf16[4,3,8,384]{3,2,1,0:T(8,128)(2,1)}), bf16[4,3,8,384]{3,2,1,0:T(8,128)(2,1)S(1)}, u32[]{:S(2)}, u32[]{:S(2)}) %all-to-all-start.3) | async-done | bytes 73760 | tf_op jit(solution)/shard_map/all_to_all | solution.py:82
  77.5 14.9 %all_gather.17 = bf16[2,256,384]{2,1,0:T(8,128)(2,1)S(1)} all-gather(bf16[2,32,384]{2,1,0:T(8,128)(2,1)S(1)} %copy_bitcast_fusion.3), channel_id=1, replica_groups=mesh['segment'=16,'cx'=4,'cz'=4,'cc'=2] {'cz','cc'}, dimensions={1}, use_global_device_ids=true | all-gather | bytes 442368 | tf_op jit(solution)/shard_map/all_gather | solution.py:85
  93.7 0.6 reshape.608
  94.3 3.3 %all-to-all-start.4 = ((f32[4,8,384]{2,1,0:T(8,128)}), f32[4,8,384]{2,1,0:T(8,128)S(1)}, u32[]{:S(2)}, u32[]{:S(2)}) async-start(f32[4,8,384]{2,1,0:T(8,128)} %reshape.608), calls=%async_computation.4 | async-start | bytes 98304 | tf_op jit(solution)/shard_map/all_to_all | solution.py:107
  97.6 5.5 %all-to-all-done.4 = f32[4,8,384]{2,1,0:T(8,128)S(1)} async-done(((f32[4,8,384]{2,1,0:T(8,128)}), f32[4,8,384]{2,1,0:T(8,128)S(1)}, u32[]{:S(2)}, u32[]{:S(2)}) %all-to-all-start.4) | async-done | bytes 49184 | tf_op jit(solution)/shard_map/all_to_all | solution.py:107
  103.1 4.8 %collective-permute-start = (bf16[8,1536]{1,0:T(8,128)(2,1)S(1)}, bf16[8,1536]{1,0:T(8,128)(2,1)S(1)}, u32[]{:S(2)}, u32[]{:S(2)}) collective-permute-start(bf16[8,1536]{1,0:T(8,128)(2,1)S(1)} %fusion.104), channel_id=1, source_target_pairs={{0,32},{32,64},{64,96},{96,128},{128,160},{160,192},{192,224},{224... | collective-permute-start | bytes 73736 | tf_op jit(solution)/shard_map/ppermute | solution.py:127
  109.9 1.1 collective-permute-done
  111.5 8.0 %all_to_all.45 = bf16[4,3,8,384]{3,2,1,0:T(8,128)(2,1)S(1)} all-to-all(bf16[4,3,8,384]{3,2,1,0:T(8,128)(2,1)S(1)} %maximum_bitcast_fusion.3), channel_id=1, replica_groups=mesh['segment'=16,'cx'=4,'cz'=4,'cc'=2] {'cx'}, dimensions={0} | all-to-all | bytes 147456 | tf_op jit(solution)/shard_map/all_to_all | solution.py:82
  119.5 14.9 %all_gather.18 = bf16[2,256,384]{2,1,0:T(8,128)(2,1)S(1)} all-gather(bf16[2,32,384]{2,1,0:T(8,128)(2,1)S(1)} %copy_bitcast_fusion.2), channel_id=1, replica_groups=mesh['segment'=16,'cx'=4,'cz'=4,'cc'=2] {'cz','cc'}, dimensions={1}, use_global_device_ids=true | all-gather | bytes 442368 | tf_op jit(solution)/shard_map/all_gather | solution.py:85
  135.7 7.9 %all_to_all.46 = f32[4,8,384]{2,1,0:T(8,128)S(1)} all-to-all(f32[4,8,384]{2,1,0:T(8,128)S(1)} %reshape.612), channel_id=1, replica_groups=mesh['segment'=16,'cx'=4,'cz'=4,'cc'=2] {'cx'}, dimensions={0} | all-to-all | bytes 98304 | tf_op jit(solution)/shard_map/all_to_all | solution.py:107
  144.1 8.0 %all_to_all.47 = bf16[4,3,8,384]{3,2,1,0:T(8,128)(2,1)S(1)} all-to-all(bf16[4,3,8,384]{3,2,1,0:T(8,128)(2,1)S(1)} %maximum_bitcast_fusion.4), channel_id=1, replica_groups=mesh['segment'=16,'cx'=4,'cz'=4,'cc'=2] {'cx'}, dimensions={0} | all-to-all | bytes 147456 | tf_op jit(solution)/shard_map/all_to_all | solution.py:82
  152.1 15.2 %all_gather.19 = bf16[2,256,384]{2,1,0:T(8,128)(2,1)S(1)} all-gather(bf16[2,32,384]{2,1,0:T(8,128)(2,1)S(1)} %copy_bitcast_fusion.1), channel_id=1, replica_groups=mesh['segment'=16,'cx'=4,'cz'=4,'cc'=2] {'cz','cc'}, dimensions={1}, use_global_device_ids=true | all-gather | bytes 442368 | tf_op jit(solution)/shard_map/all_gather | solution.py:85
  169.3 3.3 %all-to-all-start.8 = ((f32[4,8,384]{2,1,0:T(8,128)}), f32[4,8,384]{2,1,0:T(8,128)S(1)}, u32[]{:S(2)}, u32[]{:S(2)}) async-start(f32[4,8,384]{2,1,0:T(8,128)} %reshape.615), calls=%async_computation.8 | async-start | bytes 98304 | tf_op jit(solution)/shard_map/all_to_all | solution.py:107
  172.6 5.5 %all-to-all-done.8 = f32[4,8,384]{2,1,0:T(8,128)S(1)} async-done(((f32[4,8,384]{2,1,0:T(8,128)}), f32[4,8,384]{2,1,0:T(8,128)S(1)}, u32[]{:S(2)}, u32[]{:S(2)}) %all-to-all-start.8) | async-done | bytes 49184 | tf_op jit(solution)/shard_map/all_to_all | solution.py:107
  (116 shorter events, 12.9 us)
Async XLA Ops:
  0.0 0.7 copy-start.8
  0.0 2.6 %copy-start.4 = (f32[1,2,1536]{2,1,0:T(2,128)S(1)}, f32[1,2,1536]{2,1,0:T(2,128)}, u32[]{:S(2)}) copy-start(f32[1,2,1536]{2,1,0:T(2,128)} %param.14) | copy-start | bytes 36868
  0.0 2.7 %copy-start.5 = (f32[1,2,1536]{2,1,0:T(2,128)S(1)}, f32[1,2,1536]{2,1,0:T(2,128)}, u32[]{:S(2)}) copy-start(f32[1,2,1536]{2,1,0:T(2,128)} %param.15) | copy-start | bytes 36868
  0.0 3.4 %copy-start = (bf16[2,8,1536]{2,1,0:T(8,128)(2,1)S(1)}, bf16[2,8,1536]{2,1,0:T(8,128)(2,1)}, u32[]{:S(2)}) copy-start(bf16[2,8,1536]{2,1,0:T(8,128)(2,1)} %param.10) | copy-start | bytes 147460
  2.6 0.8 copy-start.3
  3.4 0.7 copy-start.6
  4.5 7.2 %copy-start.2 = (bf16[1,2,2,8,1536]{4,3,2,1,0:T(8,128)(2,1)S(1)}, bf16[1,2,2,8,1536]{4,3,2,1,0:T(8,128)(2,1)}, u32[]{:S(2)}) copy-start(bf16[1,2,2,8,1536]{4,3,2,1,0:T(8,128)(2,1)} %param.18) | copy-start | bytes 294916
  5.1 6.5 %copy-start.1 = (bf16[1,2,2,8,1536]{4,3,2,1,0:T(8,128)(2,1)S(1)}, bf16[1,2,2,8,1536]{4,3,2,1,0:T(8,128)(2,1)}, u32[]{:S(2)}) copy-start(bf16[1,2,2,8,1536]{4,3,2,1,0:T(8,128)(2,1)} %param.19) | copy-start | bytes 294916
  5.1 10.1 %all-to-all-start = ((bf16[4,3,8,384]{3,2,1,0:T(8,128)(2,1)}), bf16[4,3,8,384]{3,2,1,0:T(8,128)(2,1)S(1)}, u32[]{:S(2)}, u32[]{:S(2)}) async-start(bf16[4,3,8,384]{3,2,1,0:T(8,128)(2,1)} %maximum_bitcast_fusion.1), calls=%async_computation | async-start | bytes 147456 | tf_op jit(solution)/shard_map/all_to_all | solution.py:82
  15.2 24.3 %all-to-all-start.1 = ((bf16[4,2,2,8,384]{4,3,1,2,0:T(8,128)(2,1)}), bf16[4,2,2,8,384]{4,3,1,2,0:T(8,128)(2,1)S(1)}, u32[]{:S(2)}, u32[]{:S(2)}) async-start(bf16[4,2,2,8,384]{4,3,1,2,0:T(8,128)(2,1)} %copy.78), calls=%async_computation.1 | async-start | bytes 196608 | tf_op jit(solution)/shard_map/all_to_all | solution.py:51
  57.0 4.9 %copy-start.7 = (f32[1,2,1536]{2,1,0:T(2,128)S(1)}, f32[1,2,1536]{2,1,0:T(2,128)}, u32[]{:S(2)}) copy-start(f32[1,2,1536]{2,1,0:T(2,128)} %param.17) | copy-start | bytes 36868
  57.0 10.4 %all-to-all-start.2 = ((f32[4,8,384]{2,1,0:T(8,128)}), f32[4,8,384]{2,1,0:T(8,128)S(1)}, u32[]{:S(2)}, u32[]{:S(2)}) async-start(f32[4,8,384]{2,1,0:T(8,128)} %reshape.603), calls=%async_computation.2 | async-start | bytes 98304 | tf_op jit(solution)/shard_map/all_to_all | solution.py:107
  68.6 8.9 %all-to-all-start.3 = ((bf16[4,3,8,384]{3,2,1,0:T(8,128)(2,1)}), bf16[4,3,8,384]{3,2,1,0:T(8,128)(2,1)S(1)}, u32[]{:S(2)}, u32[]{:S(2)}) async-start(bf16[4,3,8,384]{3,2,1,0:T(8,128)(2,1)} %maximum_bitcast_fusion.2), calls=%async_computation.3 | async-start | bytes 147456 | tf_op jit(solution)/shard_map/all_to_all | solution.py:82
  94.3 8.8 %all-to-all-start.4 = ((f32[4,8,384]{2,1,0:T(8,128)}), f32[4,8,384]{2,1,0:T(8,128)S(1)}, u32[]{:S(2)}, u32[]{:S(2)}) async-start(f32[4,8,384]{2,1,0:T(8,128)} %reshape.608), calls=%async_computation.4 | async-start | bytes 98304 | tf_op jit(solution)/shard_map/all_to_all | solution.py:107
  103.1 7.8 %collective-permute-start = (bf16[8,1536]{1,0:T(8,128)(2,1)S(1)}, bf16[8,1536]{1,0:T(8,128)(2,1)S(1)}, u32[]{:S(2)}, u32[]{:S(2)}) collective-permute-start(bf16[8,1536]{1,0:T(8,128)(2,1)S(1)} %fusion.104), channel_id=1, source_target_pairs={{0,32},{32,64},{64,96},{96,128},{128,160},{160,192},{192,224},{224... | collective-permute-start | bytes 73736 | tf_op jit(solution)/shard_map/ppermute | solution.py:127
  169.3 8.8 %all-to-all-start.8 = ((f32[4,8,384]{2,1,0:T(8,128)}), f32[4,8,384]{2,1,0:T(8,128)S(1)}, u32[]{:S(2)}, u32[]{:S(2)}) async-start(f32[4,8,384]{2,1,0:T(8,128)} %reshape.615), calls=%async_computation.8 | async-start | bytes 98304 | tf_op jit(solution)/shard_map/all_to_all | solution.py:107
where the time goes:
time: 180 us; the launch traced here: 179 us
  blocking collectives  105 us (58%)
  starting transfers between devices  27.2 us (15%)
  waiting for transfers between devices  24.7 us (14%)
  local copies, waits for them, and re-layouts  8.84 us (5%)
  between operations  7.15 us (4%)
  other arithmetic  3.88 us (2%)
  matrix products  2.12 us (1%)
    all_gather x4, blocking collectives, layer(): near_kv = lax.all_gather(near_kv, TOKEN_AXES, axis=1, tiled=True)  65.2 us
    all_to_all x2, blocking collectives, layer(): mine = lax.all_to_all(packed, HEAD_AXIS, 0, 0)  16.1 us
    all_to_all x3, waiting for transfers between devices, layer(): back = lax.all_to_all(attended, HEAD_AXIS, 0, 0)  15.8 us
    all_gather x1, blocking collectives, gather_head_group(): return lax.all_gather(mine, TOKEN_AXES, axis=mine.ndim - 2, tiled=True)  15.5 us
    all_to_all x3, starting transfers between devices, layer(): back = lax.all_to_all(attended, HEAD_AXIS, 0, 0)  11.4 us
    all_to_all x1, blocking collectives, layer(): back = lax.all_to_all(attended, HEAD_AXIS, 0, 0)  7.9 us
    all_to_all x2, waiting for transfers between devices, layer(): mine = lax.all_to_all(packed, HEAD_AXIS, 0, 0)  7.79 us
    all_to_all x2, starting transfers between devices, layer(): mine = lax.all_to_all(packed, HEAD_AXIS, 0, 0)  7.71 us
  transfers between devices with their start and end apart: 7, of which 6 were waited for; matrix products, arithmetic and copies ran while one was open for 1% of the time, Pallas kernels for 0%

commit v1 on v0

--- a/solution.py
+++ b/solution.py
@@ -10,6 +10,11 @@
 HEAD_AXIS = "cx"
 TOKEN_AXES = ("cz", "cc")
 CTX_AXES = ("cx", "cz", "cc")
+
+
+def exchange_gather(array, mesh_axis, d):
+    stack = jnp.stack([array] * lax.axis_size(mesh_axis))
+    return jnp.concatenate(lax.all_to_all(stack, mesh_axis, 0, 0), axis=d)
 
 
 def head_norm(values):
@@ -82,7 +87,7 @@
         mine = lax.all_to_all(packed, HEAD_AXIS, 0, 0)
         local_q = mine[:, 0].reshape(groups * rows, group_heads, HD)
         near_kv = jnp.moveaxis(mine[:, 1:], 0, 1).reshape(2, groups * rows, group_width)
-        near_kv = lax.all_gather(near_kv, TOKEN_AXES, axis=1, tiled=True)
+        near_kv = exchange_gather(near_kv, TOKEN_AXES, 1)
         keys = jnp.concatenate([near_kv[0], far_kv[0]], axis=0)
         values = jnp.concatenate([near_kv[1], far_kv[1]], axis=0)
         key_count = keys.shape[0]

time: 180 us -> 193 us (1.072)
  the two profiles are of different devices: /device:TPU:32 before, /device:TPU:24 now
where the time goes in v1:
time: 193 us; the launch traced here: 192 us
  waiting for transfers between devices  70.3 us (36%)
  blocking collectives  56 us (29%)
  starting transfers between devices  43 us (22%)
  local copies, waits for them, and re-layouts  10.2 us (5%)
  between operations  7.21 us (4%)
  other arithmetic  3.26 us (2%)
  matrix products  2.09 us (1%)
    all_to_all x4, waiting for transfers between devices, exchange_gather(): return jnp.concatenate(lax.all_to_all(stack, mesh_axis, 0, 0), axis=d)  44.4 us
    all_to_all x3, blocking collectives, layer(): mine = lax.all_to_all(packed, HEAD_AXIS, 0, 0)  24.1 us
    all_gather x1, blocking collectives, gather_head_group(): return lax.all_gather(mine, TOKEN_AXES, axis=mine.ndim - 2, tiled=True)  24 us
    all_to_all x4, starting transfers between devices, exchange_gather(): return jnp.concatenate(lax.all_to_all(stack, mesh_axis, 0, 0), axis=d)  22.1 us
    all_to_all x3, waiting for transfers between devices, layer(): back = lax.all_to_all(attended, HEAD_AXIS, 0, 0)  15.8 us
    all_to_all x3, starting transfers between devices, layer(): back = lax.all_to_all(attended, HEAD_AXIS, 0, 0)  9.95 us
    all_to_all x1, blocking collectives, layer(): back = lax.all_to_all(attended, HEAD_AXIS, 0, 0)  7.9 us
    all_to_all x1, waiting for transfers between devices, gather_head_group(): mine = lax.all_to_all(parts, HEAD_AXIS, 0, 0)  5.75 us
  transfers between devices with their start and end apart: 10, of which 9 were waited for; matrix products, arithmetic and copies ran while one was open for 1% of the time, Pallas kernels for 0%

profile of v1, /device:TPU:24, one launch (start us, length us, event | category | flops | bytes accessed | tf_op | source)
XLA Modules:
  0.0 192.1 jit_solution(8899086676299660059)
XLA Ops:
  5.1 4.4 %all-to-all-start = ((bf16[4,3,8,384]{3,2,1,0:T(8,128)(2,1)}), bf16[4,3,8,384]{3,2,1,0:T(8,128)(2,1)S(1)}, u32[]{:S(2)}, u32[]{:S(2)}) async-start(bf16[4,3,8,384]{3,2,1,0:T(8,128)(2,1)} %maximum_bitcast_fusion.1), calls=%async_computation | async-start | bytes 147456 | tf_op jit(solution)/shard_map/all_to_all | solution.py:87
  12.4 2.8 %all-to-all-done = bf16[4,3,8,384]{3,2,1,0:T(8,128)(2,1)S(1)} async-done(((bf16[4,3,8,384]{3,2,1,0:T(8,128)(2,1)}), bf16[4,3,8,384]{3,2,1,0:T(8,128)(2,1)S(1)}, u32[]{:S(2)}, u32[]{:S(2)}) %all-to-all-start) | async-done | bytes 73760 | tf_op jit(solution)/shard_map/all_to_all | solution.py:87
  15.2 3.3 %all-to-all-start.2 = ((bf16[4,2,2,8,384]{4,3,1,2,0:T(8,128)(2,1)}), bf16[4,2,2,8,384]{4,3,1,2,0:T(8,128)(2,1)S(1)}, u32[]{:S(2)}, u32[]{:S(2)}) async-start(bf16[4,2,2,8,384]{4,3,1,2,0:T(8,128)(2,1)} %copy.95), calls=%async_computation.2 | async-start | bytes 196608 | tf_op jit(solution)/shard_map/all_to_all | solution.py:56
  18.5 5.8 %all-to-all-done.2 = bf16[4,2,2,8,384]{4,3,1,2,0:T(8,128)(2,1)S(1)} async-done(((bf16[4,2,2,8,384]{4,3,1,2,0:T(8,128)(2,1)}), bf16[4,2,2,8,384]{4,3,1,2,0:T(8,128)(2,1)S(1)}, u32[]{:S(2)}, u32[]{:S(2)}) %all-to-all-start.2) | async-done | bytes 98336 | tf_op jit(solution)/shard_map/all_to_all | solution.py:56
  25.1 10.3 %all-to-all-start.1 = ((bf16[8,2,32,384]{3,2,1,0:T(8,128)(2,1)}), bf16[8,2,32,384]{3,2,1,0:T(8,128)(2,1)S(1)}, u32[]{:S(2)}, u32[]{:S(2)}) async-start(bf16[8,2,32,384]{3,2,1,0:T(8,128)(2,1)} %stack.80), calls=%async_computation.1 | async-start | bytes 786432 | tf_op jit(solution)/shard_map/all_to_all | solution.py:17
  35.4 24.0 %all_gather.3 = bf16[2,2,256,384]{3,2,1,0:T(8,128)(2,1)S(1)} all-gather(bf16[2,2,32,384]{3,2,1,0:T(8,128)(2,1)S(1)} %bitcast.213), channel_id=1, replica_groups=mesh['segment'=16,'cx'=4,'cz'=4,'cc'=2] {'cz','cc'}, dimensions={2}, use_global_device_ids=true | all-gather | bytes 884736 | tf_op jit(solution)/shard_map/all_gather | solution.py:59
  61.6 3.4 %all-to-all-start.3 = ((f32[4,8,384]{2,1,0:T(8,128)}), f32[4,8,384]{2,1,0:T(8,128)S(1)}, u32[]{:S(2)}, u32[]{:S(2)}) async-start(f32[4,8,384]{2,1,0:T(8,128)} %reshape.631), calls=%async_computation.3 | async-start | bytes 98304 | tf_op jit(solution)/shard_map/all_to_all | solution.py:112
  65.7 4.8 %all-to-all-done.3 = f32[4,8,384]{2,1,0:T(8,128)S(1)} async-done(((f32[4,8,384]{2,1,0:T(8,128)}), f32[4,8,384]{2,1,0:T(8,128)S(1)}, u32[]{:S(2)}, u32[]{:S(2)}) %all-to-all-start.3) | async-done | bytes 49184 | tf_op jit(solution)/shard_map/all_to_all | solution.py:112
  71.1 8.0 %all_to_all.65 = bf16[4,3,8,384]{3,2,1,0:T(8,128)(2,1)S(1)} all-to-all(bf16[4,3,8,384]{3,2,1,0:T(8,128)(2,1)S(1)} %maximum_bitcast_fusion.2), channel_id=1, replica_groups=mesh['segment'=16,'cx'=4,'cz'=4,'cc'=2] {'cx'}, dimensions={0} | all-to-all | bytes 147456 | tf_op jit(solution)/shard_map/all_to_all | solution.py:87
  79.9 4.9 %all-to-all-start.5 = ((bf16[8,2,32,384]{3,2,1,0:T(8,128)(2,1)}), bf16[8,2,32,384]{3,2,1,0:T(8,128)(2,1)S(1)}, u32[]{:S(2)}, u32[]{:S(2)}) async-start(bf16[8,2,32,384]{3,2,1,0:T(8,128)(2,1)} %stack.88), calls=%async_computation.5 | async-start | bytes 786432 | tf_op jit(solution)/shard_map/all_to_all | solution.py:17
  85.5 14.1 %all-to-all-done.5 = bf16[8,2,32,384]{3,2,1,0:T(8,128)(2,1)S(1)} async-done(((bf16[8,2,32,384]{3,2,1,0:T(8,128)(2,1)}), bf16[8,2,32,384]{3,2,1,0:T(8,128)(2,1)S(1)}, u32[]{:S(2)}, u32[]{:S(2)}) %all-to-all-start.5) | async-done | bytes 393248 | tf_op jit(solution)/shard_map/all_to_all | solution.py:17
  101.1 3.3 %all-to-all-start.6 = ((f32[4,8,384]{2,1,0:T(8,128)}), f32[4,8,384]{2,1,0:T(8,128)S(1)}, u32[]{:S(2)}, u32[]{:S(2)}) async-start(f32[4,8,384]{2,1,0:T(8,128)} %reshape.636), calls=%async_computation.6 | async-start | bytes 98304 | tf_op jit(solution)/shard_map/all_to_all | solution.py:112
  104.4 5.5 %all-to-all-done.6 = f32[4,8,384]{2,1,0:T(8,128)S(1)} async-done(((f32[4,8,384]{2,1,0:T(8,128)}), f32[4,8,384]{2,1,0:T(8,128)S(1)}, u32[]{:S(2)}, u32[]{:S(2)}) %all-to-all-start.6) | async-done | bytes 49184 | tf_op jit(solution)/shard_map/all_to_all | solution.py:112
  109.9 3.2 %collective-permute-start = (bf16[8,1536]{1,0:T(8,128)(2,1)S(1)}, bf16[8,1536]{1,0:T(8,128)(2,1)S(1)}, u32[]{:S(2)}, u32[]{:S(2)}) collective-permute-start(bf16[8,1536]{1,0:T(8,128)(2,1)S(1)} %fusion.104), channel_id=1, source_target_pairs={{0,32},{32,64},{64,96},{96,128},{128,160},{160,192},{192,224},{224... | collective-permute-start | bytes 73736 | tf_op jit(solution)/shard_map/ppermute | solution.py:132
  115.0 1.5 collective-permute-done
  117.0 8.0 %all_to_all.66 = bf16[4,3,8,384]{3,2,1,0:T(8,128)(2,1)S(1)} all-to-all(bf16[4,3,8,384]{3,2,1,0:T(8,128)(2,1)S(1)} %maximum_bitcast_fusion.3), channel_id=1, replica_groups=mesh['segment'=16,'cx'=4,'cz'=4,'cc'=2] {'cx'}, dimensions={0} | all-to-all | bytes 147456 | tf_op jit(solution)/shard_map/all_to_all | solution.py:87
  125.8 3.5 %all-to-all-start.8 = ((bf16[8,2,32,384]{3,2,1,0:T(8,128)(2,1)}), bf16[8,2,32,384]{3,2,1,0:T(8,128)(2,1)S(1)}, u32[]{:S(2)}, u32[]{:S(2)}) async-start(bf16[8,2,32,384]{3,2,1,0:T(8,128)(2,1)} %stack.93), calls=%async_computation.8 | async-start | bytes 786432 | tf_op jit(solution)/shard_map/all_to_all | solution.py:17
  129.3 15.4 %all-to-all-done.8 = bf16[8,2,32,384]{3,2,1,0:T(8,128)(2,1)S(1)} async-done(((bf16[8,2,32,384]{3,2,1,0:T(8,128)(2,1)}), bf16[8,2,32,384]{3,2,1,0:T(8,128)(2,1)S(1)}, u32[]{:S(2)}, u32[]{:S(2)}) %all-to-all-start.8) | async-done | bytes 393248 | tf_op jit(solution)/shard_map/all_to_all | solution.py:17
  145.6 7.9 %all_to_all.67 = f32[4,8,384]{2,1,0:T(8,128)S(1)} all-to-all(f32[4,8,384]{2,1,0:T(8,128)S(1)} %reshape.640), channel_id=1, replica_groups=mesh['segment'=16,'cx'=4,'cz'=4,'cc'=2] {'cx'}, dimensions={0} | all-to-all | bytes 98304 | tf_op jit(solution)/shard_map/all_to_all | solution.py:112
  154.0 8.0 %all_to_all.68 = bf16[4,3,8,384]{3,2,1,0:T(8,128)(2,1)S(1)} all-to-all(bf16[4,3,8,384]{3,2,1,0:T(8,128)(2,1)S(1)} %maximum_bitcast_fusion.4), channel_id=1, replica_groups=mesh['segment'=16,'cx'=4,'cz'=4,'cc'=2] {'cx'}, dimensions={0} | all-to-all | bytes 147456 | tf_op jit(solution)/shard_map/all_to_all | solution.py:87
  162.8 3.5 %all-to-all-start.11 = ((bf16[8,2,32,384]{3,2,1,0:T(8,128)(2,1)}), bf16[8,2,32,384]{3,2,1,0:T(8,128)(2,1)S(1)}, u32[]{:S(2)}, u32[]{:S(2)}) async-start(bf16[8,2,32,384]{3,2,1,0:T(8,128)(2,1)} %stack.98), calls=%async_computation.11 | async-start | bytes 786432 | tf_op jit(solution)/shard_map/all_to_all | solution.py:17
  166.3 14.8 %all-to-all-done.11 = bf16[8,2,32,384]{3,2,1,0:T(8,128)(2,1)S(1)} async-done(((bf16[8,2,32,384]{3,2,1,0:T(8,128)(2,1)}), bf16[8,2,32,384]{3,2,1,0:T(8,128)(2,1)S(1)}, u32[]{:S(2)}, u32[]{:S(2)}) %all-to-all-start.11) | async-done | bytes 393248 | tf_op jit(solution)/shard_map/all_to_all | solution.py:17
  182.6 3.3 %all-to-all-start.12 = ((f32[4,8,384]{2,1,0:T(8,128)}), f32[4,8,384]{2,1,0:T(8,128)S(1)}, u32[]{:S(2)}, u32[]{:S(2)}) async-start(f32[4,8,384]{2,1,0:T(8,128)} %reshape.643), calls=%async_computation.12 | async-start | bytes 98304 | tf_op jit(solution)/shard_map/all_to_all | solution.py:112
  186.0 5.5 %all-to-all-done.12 = f32[4,8,384]{2,1,0:T(8,128)S(1)} async-done(((f32[4,8,384]{2,1,0:T(8,128)}), f32[4,8,384]{2,1,0:T(8,128)S(1)}, u32[]{:S(2)}, u32[]{:S(2)}) %all-to-all-start.12) | async-done | bytes 49184 | tf_op jit(solution)/shard_map/all_to_all | solution.py:112
  (123 shorter events, 15.6 us)
Async XLA Ops:
  0.0 0.7 copy-start.8
  0.0 2.6 %copy-start.4 = (f32[1,2,1536]{2,1,0:T(2,128)S(1)}, f32[1,2,1536]{2,1,0:T(2,128)}, u32[]{:S(2)}) copy-start(f32[1,2,1536]{2,1,0:T(2,128)} %param.14) | copy-start | bytes 36868
  0.0 2.7 %copy-start.5 = (f32[1,2,1536]{2,1,0:T(2,128)S(1)}, f32[1,2,1536]{2,1,0:T(2,128)}, u32[]{:S(2)}) copy-start(f32[1,2,1536]{2,1,0:T(2,128)} %param.15) | copy-start | bytes 36868
  0.0 3.4 %copy-start = (bf16[2,8,1536]{2,1,0:T(8,128)(2,1)S(1)}, bf16[2,8,1536]{2,1,0:T(8,128)(2,1)}, u32[]{:S(2)}) copy-start(bf16[2,8,1536]{2,1,0:T(8,128)(2,1)} %param.10) | copy-start | bytes 147460
  2.6 0.8 copy-start.3
  3.4 0.7 copy-start.6
  4.5 7.2 %copy-start.2 = (bf16[1,2,2,8,1536]{4,3,2,1,0:T(8,128)(2,1)S(1)}, bf16[1,2,2,8,1536]{4,3,2,1,0:T(8,128)(2,1)}, u32[]{:S(2)}) copy-start(bf16[1,2,2,8,1536]{4,3,2,1,0:T(8,128)(2,1)} %param.18) | copy-start | bytes 294916
  5.1 6.5 %copy-start.1 = (bf16[1,2,2,8,1536]{4,3,2,1,0:T(8,128)(2,1)S(1)}, bf16[1,2,2,8,1536]{4,3,2,1,0:T(8,128)(2,1)}, u32[]{:S(2)}) copy-start(bf16[1,2,2,8,1536]{4,3,2,1,0:T(8,128)(2,1)} %param.19) | copy-start | bytes 294916
  5.1 10.1 %all-to-all-start = ((bf16[4,3,8,384]{3,2,1,0:T(8,128)(2,1)}), bf16[4,3,8,384]{3,2,1,0:T(8,128)(2,1)S(1)}, u32[]{:S(2)}, u32[]{:S(2)}) async-start(bf16[4,3,8,384]{3,2,1,0:T(8,128)(2,1)} %maximum_bitcast_fusion.1), calls=%async_computation | async-start | bytes 147456 | tf_op jit(solution)/shard_map/all_to_all | solution.py:87
  15.2 9.1 %all-to-all-start.2 = ((bf16[4,2,2,8,384]{4,3,1,2,0:T(8,128)(2,1)}), bf16[4,2,2,8,384]{4,3,1,2,0:T(8,128)(2,1)S(1)}, u32[]{:S(2)}, u32[]{:S(2)}) async-start(bf16[4,2,2,8,384]{4,3,1,2,0:T(8,128)(2,1)} %copy.95), calls=%async_computation.2 | async-start | bytes 196608 | tf_op jit(solution)/shard_map/all_to_all | solution.py:56
  25.1 35.1 %all-to-all-start.1 = ((bf16[8,2,32,384]{3,2,1,0:T(8,128)(2,1)}), bf16[8,2,32,384]{3,2,1,0:T(8,128)(2,1)S(1)}, u32[]{:S(2)}, u32[]{:S(2)}) async-start(bf16[8,2,32,384]{3,2,1,0:T(8,128)(2,1)} %stack.80), calls=%async_computation.1 | async-start | bytes 786432 | tf_op jit(solution)/shard_map/all_to_all | solution.py:17
  61.6 3.4 %copy-start.7 = (f32[1,2,1536]{2,1,0:T(2,128)S(1)}, f32[1,2,1536]{2,1,0:T(2,128)}, u32[]{:S(2)}) copy-start(f32[1,2,1536]{2,1,0:T(2,128)} %param.17) | copy-start | bytes 36868
  61.6 8.9 %all-to-all-start.3 = ((f32[4,8,384]{2,1,0:T(8,128)}), f32[4,8,384]{2,1,0:T(8,128)S(1)}, u32[]{:S(2)}, u32[]{:S(2)}) async-start(f32[4,8,384]{2,1,0:T(8,128)} %reshape.631), calls=%async_computation.3 | async-start | bytes 98304 | tf_op jit(solution)/shard_map/all_to_all | solution.py:112
  79.9 19.7 %all-to-all-start.5 = ((bf16[8,2,32,384]{3,2,1,0:T(8,128)(2,1)}), bf16[8,2,32,384]{3,2,1,0:T(8,128)(2,1)S(1)}, u32[]{:S(2)}, u32[]{:S(2)}) async-start(bf16[8,2,32,384]{3,2,1,0:T(8,128)(2,1)} %stack.88), calls=%async_computation.5 | async-start | bytes 786432 | tf_op jit(solution)/shard_map/all_to_all | solution.py:17
  101.1 8.8 %all-to-all-start.6 = ((f32[4,8,384]{2,1,0:T(8,128)}), f32[4,8,384]{2,1,0:T(8,128)S(1)}, u32[]{:S(2)}, u32[]{:S(2)}) async-start(f32[4,8,384]{2,1,0:T(8,128)} %reshape.636), calls=%async_computation.6 | async-start | bytes 98304 | tf_op jit(solution)/shard_map/all_to_all | solution.py:112
  109.9 6.6 %collective-permute-start = (bf16[8,1536]{1,0:T(8,128)(2,1)S(1)}, bf16[8,1536]{1,0:T(8,128)(2,1)S(1)}, u32[]{:S(2)}, u32[]{:S(2)}) collective-permute-start(bf16[8,1536]{1,0:T(8,128)(2,1)S(1)} %fusion.104), channel_id=1, source_target_pairs={{0,32},{32,64},{64,96},{96,128},{128,160},{160,192},{192,224},{224... | collective-permute-start | bytes 73736 | tf_op jit(solution)/shard_map/ppermute | solution.py:132
  125.8 18.9 %all-to-all-start.8 = ((bf16[8,2,32,384]{3,2,1,0:T(8,128)(2,1)}), bf16[8,2,32,384]{3,2,1,0:T(8,128)(2,1)S(1)}, u32[]{:S(2)}, u32[]{:S(2)}) async-start(bf16[8,2,32,384]{3,2,1,0:T(8,128)(2,1)} %stack.93), calls=%async_computation.8 | async-start | bytes 786432 | tf_op jit(solution)/shard_map/all_to_all | solution.py:17
  162.8 18.3 %all-to-all-start.11 = ((bf16[8,2,32,384]{3,2,1,0:T(8,128)(2,1)}), bf16[8,2,32,384]{3,2,1,0:T(8,128)(2,1)S(1)}, u32[]{:S(2)}, u32[]{:S(2)}) async-start(bf16[8,2,32,384]{3,2,1,0:T(8,128)(2,1)} %stack.98), calls=%async_computation.11 | async-start | bytes 786432 | tf_op jit(solution)/shard_map/all_to_all | solution.py:17
  182.6 8.8 %all-to-all-start.12 = ((f32[4,8,384]{2,1,0:T(8,128)}), f32[4,8,384]{2,1,0:T(8,128)S(1)}, u32[]{:S(2)}, u32[]{:S(2)}) async-start(f32[4,8,384]{2,1,0:T(8,128)} %reshape.643), calls=%async_computation.12 | async-start | bytes 98304 | tf_op jit(solution)/shard_map/all_to_all | solution.py:112
